TPU v7x, 512 devices: a whole 4x4x16 slice. The times are simulated.
512 devices in a mesh: aux: 16 (over z), pair: 32 (over y, x, core).
Axes of the slice: x: 4, y: 4, z: 16, core: 2. Of those that a mesh axis runs over, the one named last changes fastest.
Arguments:
- b_tensor: bfloat16 [2560, 262144], P('aux', 'pair'), may hold values from -0.0625 to 0.0625
- eps_occ: float32 [256], replicated, may hold values from -1 to -0.3
- eps_vir: float32 [1024], replicated, may hold values from 0.05 to 3
- trial: bfloat16 [32, 262144], P(None, 'pair'), may hold values from -6 to 6
Outputs:
- trial_next: float32 [32, 262144], P(None, 'pair')
- residual: bfloat16 [32, 262144], P(None, 'pair')
- subspace: float32 [32, 32], replicated
All inputs are finite; a program needn't handle non-finite values.
Results may differ from a plain program's by a relative error of at most 0.028.
Values may be sent and summed in bfloat16 or wider, within the bound.
No kernel may reach another device: no remote copies, remote signals or barrier semaphores. Data moves between devices by JAX's collectives and lax.ppermute only.
A program may use at most 64 MiB of HBM per device.

v0:
```python
import jax
import jax.numpy as jnp
from jax import lax
from jax.sharding import PartitionSpec as P

ITERS = 2
HIGHEST_PRECISION = lax.Precision.HIGHEST


def correlation_of(first_rows, second_rows, precision=HIGHEST_PRECISION):
    return lax.dot_general(
        first_rows,
        second_rows,
        (((1,), (1,)), ((), ())),
        precision=precision,
        preferred_element_type=jnp.float32,
    )


def product(first_mat, second_mat):
    return jnp.dot(
        first_mat, second_mat, precision=HIGHEST_PRECISION, preferred_element_type=jnp.float32
    )


def pair_sum(matrices):
    return lax.all_gather(matrices, "pair").sum(0)


def aux_sum(terms):
    n_aux = lax.axis_size("aux")
    rows, cols = terms.shape
    pieces = terms.reshape(rows, n_aux, cols // n_aux)
    pieces = lax.all_to_all(pieces, "aux", 1, 1, tiled=True)
    mine = pieces.astype(jnp.float32).sum(1)
    return lax.all_gather(mine, "aux", axis=1, tiled=True)


def inverse_factor(gram_now):
    lower_tri = jnp.linalg.cholesky(gram_now)
    return lax.linalg.triangular_solve(
        lower_tri, jnp.eye(gram_now.shape[0], dtype=jnp.float32), left_side=True, lower=True
    )


def on_device(b_tensor, eps_occ, eps_vir, trial):
    block_cols = b_tensor.shape[1]
    npair_all = eps_occ.shape[0] * eps_vir.shape[0]
    k = trial.shape[0]
    everything = (eps_vir[None, :] - eps_occ[:, None]).reshape(npair_all)
    diagonal = lax.dynamic_slice_in_dim(everything, lax.axis_index("pair") * block_cols, block_cols)
    diag_row = diagonal[None, :]
    trial_now = trial
    for iteration in range(ITERS):
        if iteration == 0:
            gram_part = correlation_of(trial_now, trial_now, None)
            cross_part = correlation_of(b_tensor, trial_now, None)
        else:
            gram_part = correlation_of(trial_now, trial_now)
            cross_part = correlation_of(b_tensor.astype(jnp.float32), trial_now)
        summed = pair_sum(jnp.concatenate([gram_part / npair_all, cross_part], axis=0))
        inverse = inverse_factor(summed[:k])
        basis_now = product(inverse, trial_now.astype(jnp.float32))
        projected = lax.dot_general(
            summed[k:],
            inverse,
            (((1,), (1,)), ((), ())),
            precision=HIGHEST_PRECISION,
            preferred_element_type=jnp.float32,
        )
        projected_low = projected.astype(jnp.bfloat16)
        term = lax.dot_general(
            projected_low, b_tensor, (((0,), (0,)), ((), ())), preferred_element_type=jnp.float32
        ).astype(jnp.bfloat16)
        image_now = aux_sum(term) + diag_row * basis_now
        subspace = pair_sum(correlation_of(image_now, basis_now) / npair_all)
        residual = image_now - product(subspace, basis_now)
        trial_now = basis_now - residual / diag_row
    return (trial_now, residual.astype(jnp.bfloat16), subspace)


def solution(mesh):
    in_specs = (P("aux", "pair"), P(), P(), P(None, "pair"))
    out_specs = (P(None, "pair"), P(None, "pair"), P())
    return jax.shard_map(
        on_device, mesh=mesh, in_specs=in_specs, out_specs=out_specs, check_vma=False
    )
```

profile of v0, /device:TPU:1, one launch (start us, length us, event | category | flops | bytes accessed | tf_op | source)
XLA Modules:
  0.0 371.0 jit_solution(16617916019839826232)
XLA Ops:
  7.2 1.6 convolution_multiply_fusion.3
  9.2 2.0 fusion.19
  11.3 31.4 %all-gather.4 = f32[32,192,32]{1,2,0:T(8,128)} all-gather(f32[1,192,32]{1,2,0:T(8,128)S(1)} %maximum_bitcast_fusion), channel_id=2, replica_groups=mesh['aux'=16,'pair'=32] {'pair'}, dimensions={0}, use_global_device_ids=true | all-gather | bytes 811008 | tf_op jit(solution)/shard_map/all_gather | solution.py:27
  42.7 1.3 reduce_sum.54
  44.1 2.9 cholesky.44
  48.4 2.4 custom-call.6
  52.2 35.2 %all_to_all.10 = bf16[32,16,512]{2,0,1:T(8,128)(2,1)S(1)} all-to-all(bf16[32,16,512]{2,0,1:T(8,128)(2,1)S(1)} %bitcast.64), channel_id=1, replica_groups=mesh['aux'=16,'pair'=32] {'aux'}, dimensions={1} | all-to-all | bytes 1048576 | tf_op jit(solution)/shard_map/all_to_all | solution.py:34
  88.3 1.2 copy.28
  90.3 1.5 fusion.20
  91.8 57.8 %all-gather.9.cloned.1.call-done = f32[32,8192]{1,0:T(8,128)} async-done(((f32[32,512]{1,0:T(8,128)}), f32[32,8192]{1,0:T(8,128)}) %all-gather.9.cloned.1.call-update) | async-done | bytes 1048592 | tf_op jit(solution)/shard_map/all_gather | solution.py:36
  149.6 2.9 convolution_multiply_fusion.2
  152.6 34.8 %all-gather.1 = f32[1024,32]{1,0:T(8,128)S(1)} all-gather(f32[32,32]{1,0:T(8,128)S(1)} %copy.14), channel_id=3, replica_groups=mesh['aux'=16,'pair'=32] {'pair'}, dimensions={0}, use_global_device_ids=true | all-gather | bytes 135168 | tf_op jit(solution)/shard_map/all_gather | solution.py:27
  187.4 3.0 fusion.1
  190.5 2.4 convolution_bitcast_fusion
  194.0 26.7 %all-gather.5 = f32[32,192,32]{1,2,0:T(8,128)} all-gather(f32[1,192,32]{1,2,0:T(8,128)S(1)} %maximum_bitcast_fusion.1), channel_id=4, replica_groups=mesh['aux'=16,'pair'=32] {'pair'}, dimensions={0}, use_global_device_ids=true | all-gather | bytes 811008 | tf_op jit(solution)/shard_map/all_gather | solution.py:27
  220.7 1.3 reduce_sum.57
  222.1 2.9 cholesky.55
  226.3 2.4 custom-call.7
  230.1 30.5 %all_to_all.11 = bf16[32,16,512]{2,0,1:T(8,128)(2,1)S(1)} all-to-all(bf16[32,16,512]{2,0,1:T(8,128)(2,1)S(1)} %bitcast.66), channel_id=1, replica_groups=mesh['aux'=16,'pair'=32] {'aux'}, dimensions={1} | all-to-all | bytes 1048576 | tf_op jit(solution)/shard_map/all_to_all | solution.py:34
  261.3 3.2 fusion.21
  264.5 57.6 %all-gather.11.cloned.1.call-done = f32[32,8192]{1,0:T(8,128)} async-done(((f32[32,512]{1,0:T(8,128)}), f32[32,8192]{1,0:T(8,128)}) %all-gather.11.cloned.1.call-update) | async-done | bytes 1048592 | tf_op jit(solution)/shard_map/all_gather | solution.py:36
  322.1 2.9 convolution_multiply_fusion
  325.1 34.8 %all-gather.3 = f32[1024,32]{1,0:T(8,128)S(1)} all-gather(f32[32,32]{1,0:T(8,128)S(1)} %copy.19), channel_id=5, replica_groups=mesh['aux'=16,'pair'=32] {'pair'}, dimensions={0}, use_global_device_ids=true | all-gather | bytes 135168 | tf_op jit(solution)/shard_map/all_gather | solution.py:27
  360.0 4.2 %fusion.18 = (bf16[32,8192]{1,0:T(8,128)(2,1)}, f32[32,8192]{1,0:T(8,128)}) fusion(f32[32,8192]{1,0:T(8,128)} %fusion.21, f32[8192]{0:T(1024)S(1)} %dynamic_slice.3, f32[32,32]{1,0:T(8,128)S(1)} %reduce_sum.59, f32[32,8192]{1,0:T(8,128)} %all-gather.11.cloned.1.call-done), kind=kOutput, calls=%fused_computation.48 | convolution fusion | flops 102236160 | bytes 3706880 | tf_op jit(solution)/shard_map/dot_general | solution.py:21
  (47 shorter events, 9.6 us)
Async XLA Ops:
  7.2 2.1 copy-start
  7.2 142.5 %all-gather.9.cloned.1.call-start = ((), (), s32[]{:S(2)}) async-start(), calls=%async_computation.2 | async-start | bytes 1114112 | tf_op jit(solution)/shard_map/all_gather | solution.py:36
  51.4 36.7 %copy-start.4 = (f32[1024]{0:T(1024)S(1)}, f32[1024]{0:T(1024)}, u32[]{:S(2)}) copy-start(f32[1024]{0:T(1024)} %param.9) | copy-start | bytes 12292
  51.4 36.7 %copy-start.5 = (f32[256]{0:T(256)S(1)}, f32[256]{0:T(256)}, u32[]{:S(2)}) copy-start(f32[256]{0:T(256)} %param.8) | copy-start | bytes 3076
  52.2 38.1 %copy-start.2 = (bf16[32,8192]{1,0:T(8,128)(2,1)S(1)}, bf16[32,8192]{1,0:T(8,128)(2,1)}, u32[]{:S(2)}) copy-start(bf16[32,8192]{1,0:T(8,128)(2,1)} %param.10) | copy-start | bytes 1572868
  88.1 234.0 %all-gather.11.cloned.1.call-start = ((), (), s32[]{:S(2)}) async-start(), calls=%async_computation.3 | async-start | bytes 1114112 | tf_op jit(solution)/shard_map/all_gather | solution.py:36
  190.5 3.4 copy-start.1
  359.9 4.2 %copy-start.3 = (f32[32,32]{1,0:T(8,128)}, f32[32,32]{1,0:T(8,128)S(1)}, u32[]{:S(2)}) copy-start(f32[32,32]{1,0:T(8,128)S(1)} %reduce_sum.59) | copy-start | bytes 12292
Sparse Core Ops, SparseCore 0:
  88.2 61.3 all-gather.8
  261.4 60.6 all-gather.10
where the time goes:
time: 372 us; the launch traced here: 371 us
  blocking collectives  193 us (52%)
  waiting for transfers between devices  115 us (31%)
  matrix products  27.3 us (7%)
  other arithmetic  17.8 us (5%)
  between operations  14.3 us (4%)
    all_gather x4, blocking collectives, pair_sum(): return lax.all_gather(matrices, 'pair').sum(0)  128 us
    all_gather x2, waiting for transfers between devices, aux_sum(): return lax.all_gather(mine, 'aux', axis=1, tiled=True)  115 us
    all_to_all x2, blocking collectives, aux_sum(): pieces = lax.all_to_all(pieces, 'aux', 1, 1, tiled=True)  65.7 us
    dot_general x6, matrix products, correlation_of(): lax.dot_general(first_rows, second_rows, (((1,), (1,)), ((), ())), precis...  12.8 us
    dot_general x4, matrix products, product(): jnp.dot(first_mat, second_mat, precision=HIGHEST_PRECISION, preferred_ele...  12 us
  transfers between devices with their start and end apart: 2, of which 2 were waited for; matrix products, arithmetic and copies ran while one was open for 2% of the time, Pallas kernels for 0%

commit v1 on v0

--- a/solution.py
+++ b/solution.py
@@ -5,6 +5,27 @@
 
 ITERS = 2
 HIGHEST_PRECISION = lax.Precision.HIGHEST
+
+
+def collect(shard, axis, dim):
+    size, index, rows = (lax.axis_size(axis), lax.axis_index(axis), shard.shape[dim])
+    ahead = [(i, (i + 1) % size) for i in range(size)]
+    backward = [(i, (i - 1) % size) for i in range(size)]
+    filled = jnp.zeros((*shard.shape[:dim], size * rows, *shard.shape[dim + 1 :]), shard.dtype)
+    filled = lax.dynamic_update_slice_in_dim(filled, shard, index * rows, axis=dim)
+    from_left = from_right = shard
+    half = size // 2
+    for step in range(1, half + 1):
+        from_left = lax.ppermute(from_left, axis, ahead)
+        filled = lax.dynamic_update_slice_in_dim(
+            filled, from_left, (index - step) % size * rows, axis=dim
+        )
+        if step < size - half:
+            from_right = lax.ppermute(from_right, axis, backward)
+            filled = lax.dynamic_update_slice_in_dim(
+                filled, from_right, (index + step) % size * rows, axis=dim
+            )
+    return filled
 
 
 def correlation_of(first_rows, second_rows, precision=HIGHEST_PRECISION):
@@ -33,7 +54,7 @@
     pieces = terms.reshape(rows, n_aux, cols // n_aux)
     pieces = lax.all_to_all(pieces, "aux", 1, 1, tiled=True)
     mine = pieces.astype(jnp.float32).sum(1)
-    return lax.all_gather(mine, "aux", axis=1, tiled=True)
+    return collect(mine, "aux", 1)
 
 
 def inverse_factor(gram_now):

time: 372 us -> 346 us (0.930)
  starting transfers between devices: 0.08 us -> 120 us
  blocking collectives: 193 us -> 126 us
  waiting for transfers between devices: 115 us -> 48.8 us
  between operations: 14.3 us -> 1.82 us
  local copies, waits for them, and re-layouts: 2.75 us -> 6.88 us
  matrix products: 27.3 us -> 23.4 us
    all_gather x2 -> x0, waiting for transfers between devices: 115 us -> none  [aux_sum(): return lax.all_gather(mine, 'aux', axis=1, tiled=True)]
    ppermute x0 -> x30, starting transfers between devices: none -> 104 us  [the longest x14 64.2 us: collect(): from_right = lax.ppermute(from_right, axis, backward)]
    all_to_all x2 -> x0, blocking collectives: 65.7 us -> none  [aux_sum(): pieces = lax.all_to_all(pieces, 'aux', 1, 1, tiled=True)]
    all_to_all x0 -> x2, waiting for transfers between devices: none -> 39 us  [aux_sum(): pieces = lax.all_to_all(pieces, 'aux', 1, 1, tiled=True)]
    all_to_all x0 -> x2, starting transfers between devices: none -> 16.6 us  [aux_sum(): pieces = lax.all_to_all(pieces, 'aux', 1, 1, tiled=True)]
    ppermute x0 -> x30, waiting for transfers between devices: none -> 9.77 us  [the longest x16 9.73 us: collect(): from_left = lax.ppermute(from_left, axis, ahead)]
  transfers between devices with their start and end apart: 2 -> 32, of which waited for: 2 -> 6; matrix products, arithmetic and copies ran while one was open for 2% -> 2% of each run, Pallas kernels for 0% -> 0%
where the time goes in v1:
time: 346 us; the launch traced here: 345 us
  blocking collectives  126 us (36%)
  starting transfers between devices  120 us (35%)
  waiting for transfers between devices  48.8 us (14%)
  matrix products  23.4 us (7%)
  other arithmetic  17.7 us (5%)
  local copies, waits for them, and re-layouts  6.88 us (2%)
    all_gather x4, blocking collectives, pair_sum(): return lax.all_gather(matrices, 'pair').sum(0)  126 us
    ppermute x14, starting transfers between devices, collect(): from_right = lax.ppermute(from_right, axis, backward)  64.2 us
    ppermute x16, starting transfers between devices, collect(): from_left = lax.ppermute(from_left, axis, ahead)  39.5 us
    all_to_all x2, waiting for transfers between devices, aux_sum(): pieces = lax.all_to_all(pieces, 'aux', 1, 1, tiled=True)  39 us
    all_to_all x2, starting transfers between devices, aux_sum(): pieces = lax.all_to_all(pieces, 'aux', 1, 1, tiled=True)  16.6 us
    dot_general x4, matrix products, product(): jnp.dot(first_mat, second_mat, precision=HIGHEST_PRECISION, preferred_ele...  11.9 us
    ppermute x16, waiting for transfers between devices, collect(): from_left = lax.ppermute(from_left, axis, ahead)  9.73 us
    dot_general x6, matrix products, correlation_of(): lax.dot_general(first_rows, second_rows, (((1,), (1,)), ((), ())), precis...  9.09 us
  transfers between devices with their start and end apart: 32, of which 6 were waited for; matrix products, arithmetic and copies ran while one was open for 2% of the time, Pallas kernels for 0%

profile of v1, /device:TPU:1, one launch (start us, length us, event | category | flops | bytes accessed | tf_op | source)
XLA Modules:
  0.0 344.6 jit_solution(12393088297308046360)
XLA Ops:
  4.7 31.4 %all-gather.4 = f32[32,192,32]{1,2,0:T(8,128)} all-gather(f32[1,192,32]{1,2,0:T(8,128)S(1)} %maximum_bitcast_fusion), channel_id=2, replica_groups=mesh['aux'=16,'pair'=32] {'pair'}, dimensions={0}, use_global_device_ids=true | all-gather | bytes 811008 | tf_op jit(solution)/shard_map/all_gather | solution.py:48
  46.4 12.5 %all-to-all-start = ((bf16[32,16,512]{2,0,1:T(8,128)(2,1)}), bf16[32,16,512]{2,0,1:T(8,128)(2,1)}, u32[]{:S(2)}, u32[]{:S(2)}) async-start(bf16[32,16,512]{2,0,1:T(8,128)(2,1)} %bitcast.63), calls=%async_computation | async-start | bytes 1048576 | tf_op jit(solution)/shard_map/all_to_all | solution.py:55
  62.8 19.2 %all-to-all-done = bf16[32,16,512]{2,0,1:T(8,128)(2,1)} async-done(((bf16[32,16,512]{2,0,1:T(8,128)(2,1)}), bf16[32,16,512]{2,0,1:T(8,128)(2,1)}, u32[]{:S(2)}, u32[]{:S(2)}) %all-to-all-start) | async-done | bytes 524320 | tf_op jit(solution)/shard_map/all_to_all | solution.py:55
  83.2 6.3 %collective-permute-start = (f32[32,512]{1,0:T(8,128)S(1)}, f32[32,512]{1,0:T(8,128)S(1)}, u32[]{:S(2)}, u32[]{:S(2)}) collective-permute-start(f32[32,512]{1,0:T(8,128)S(1)} %convert_reduce_fusion.1), channel_id=1, source_target_pairs={{0,32},{32,64},{64,96},{96,128},{128,160},{160,192},{192,224},{224... | collective-permute-start | bytes 196616 | tf_op jit(solution)/shard_map/ppermute | solution.py:19
  89.4 4.7 %collective-permute-start.1 = (f32[32,512]{1,0:T(8,128)S(1)}, f32[32,512]{1,0:T(8,128)S(1)}, u32[]{:S(2)}, u32[]{:S(2)}) collective-permute-start(f32[32,512]{1,0:T(8,128)S(1)} %convert_reduce_fusion.1), channel_id=1, source_target_pairs={{0,480},{32,0},{64,32},{96,64},{128,96},{160,128},{192,160},{224,1... | collective-permute-start | bytes 196616 | tf_op jit(solution)/shard_map/ppermute | solution.py:24
  96.2 4.6 %collective-permute-start.3 = (f32[32,512]{1,0:T(8,128)S(1)}, f32[32,512]{1,0:T(8,128)S(1)}, u32[]{:S(2)}, u32[]{:S(2)}) collective-permute-start(f32[32,512]{1,0:T(8,128)S(1)} %collective-permute-done.1), channel_id=1, source_target_pairs={{0,480},{32,0},{64,32},{96,64},{128,96},{160,128},{192,160},{224,1... | collective-permute-start | bytes 196616 | tf_op jit(solution)/shard_map/ppermute | solution.py:24
  102.7 4.6 %collective-permute-start.5 = (f32[32,512]{1,0:T(8,128)S(1)}, f32[32,512]{1,0:T(8,128)S(1)}, u32[]{:S(2)}, u32[]{:S(2)}) collective-permute-start(f32[32,512]{1,0:T(8,128)S(1)} %collective-permute-done.3), channel_id=1, source_target_pairs={{0,480},{32,0},{64,32},{96,64},{128,96},{160,128},{192,160},{224,1... | collective-permute-start | bytes 196616 | tf_op jit(solution)/shard_map/ppermute | solution.py:24
  109.3 4.6 %collective-permute-start.7 = (f32[32,512]{1,0:T(8,128)S(1)}, f32[32,512]{1,0:T(8,128)S(1)}, u32[]{:S(2)}, u32[]{:S(2)}) collective-permute-start(f32[32,512]{1,0:T(8,128)S(1)} %collective-permute-done.5), channel_id=1, source_target_pairs={{0,480},{32,0},{64,32},{96,64},{128,96},{160,128},{192,160},{224,1... | collective-permute-start | bytes 196616 | tf_op jit(solution)/shard_map/ppermute | solution.py:24
  115.9 4.6 %collective-permute-start.9 = (f32[32,512]{1,0:T(8,128)S(1)}, f32[32,512]{1,0:T(8,128)S(1)}, u32[]{:S(2)}, u32[]{:S(2)}) collective-permute-start(f32[32,512]{1,0:T(8,128)S(1)} %collective-permute-done.7), channel_id=1, source_target_pairs={{0,480},{32,0},{64,32},{96,64},{128,96},{160,128},{192,160},{224,1... | collective-permute-start | bytes 196616 | tf_op jit(solution)/shard_map/ppermute | solution.py:24
  123.0 4.6 %collective-permute-start.11 = (f32[32,512]{1,0:T(8,128)S(1)}, f32[32,512]{1,0:T(8,128)S(1)}, u32[]{:S(2)}, u32[]{:S(2)}) collective-permute-start(f32[32,512]{1,0:T(8,128)S(1)} %collective-permute-done.9), channel_id=1, source_target_pairs={{0,480},{32,0},{64,32},{96,64},{128,96},{160,128},{192,160},{224,1... | collective-permute-start | bytes 196616 | tf_op jit(solution)/shard_map/ppermute | solution.py:24
  129.6 4.6 %collective-permute-start.13 = (f32[32,512]{1,0:T(8,128)S(1)}, f32[32,512]{1,0:T(8,128)S(1)}, u32[]{:S(2)}, u32[]{:S(2)}) collective-permute-start(f32[32,512]{1,0:T(8,128)S(1)} %collective-permute-done.11), channel_id=1, source_target_pairs={{0,480},{32,0},{64,32},{96,64},{128,96},{160,128},{192,160},{224,1... | collective-permute-start | bytes 196616 | tf_op jit(solution)/shard_map/ppermute | solution.py:24
  136.2 4.2 %collective-permute-done.14 = f32[32,512]{1,0:T(8,128)S(1)} collective-permute-done((f32[32,512]{1,0:T(8,128)S(1)}, f32[32,512]{1,0:T(8,128)S(1)}, u32[]{:S(2)}, u32[]{:S(2)}) %collective-permute-start.14) | collective-permute-done | bytes 65568 | tf_op jit(solution)/shard_map/ppermute | solution.py:19
  142.6 34.6 %all-gather.1 = f32[1024,32]{1,0:T(8,128)S(1)} all-gather(f32[32,32]{1,0:T(8,128)S(1)} %copy.14), channel_id=3, replica_groups=mesh['aux'=16,'pair'=32] {'pair'}, dimensions={0}, use_global_device_ids=true | all-gather | bytes 135168 | tf_op jit(solution)/shard_map/all_gather | solution.py:48
  183.8 25.0 %all-gather.5 = f32[32,192,32]{1,2,0:T(8,128)} all-gather(f32[1,192,32]{1,2,0:T(8,128)S(1)} %maximum_bitcast_fusion.1), channel_id=4, replica_groups=mesh['aux'=16,'pair'=32] {'pair'}, dimensions={0}, use_global_device_ids=true | all-gather | bytes 811008 | tf_op jit(solution)/shard_map/all_gather | solution.py:48
  226.3 19.8 %all-to-all-done.1 = bf16[32,16,512]{2,0,1:T(8,128)(2,1)S(1)} async-done(((bf16[32,16,512]{2,0,1:T(8,128)(2,1)}), bf16[32,16,512]{2,0,1:T(8,128)(2,1)S(1)}, u32[]{:S(2)}, u32[]{:S(2)}) %all-to-all-start.1) | async-done | bytes 524320 | tf_op jit(solution)/shard_map/all_to_all | solution.py:55
  246.2 6.4 %collective-permute-start.15 = (f32[32,512]{1,0:T(8,128)S(1)}, f32[32,512]{1,0:T(8,128)S(1)}, u32[]{:S(2)}, u32[]{:S(2)}) collective-permute-start(f32[32,512]{1,0:T(8,128)S(1)} %convert_reduce_fusion), channel_id=1, source_target_pairs={{0,32},{32,64},{64,96},{96,128},{128,160},{160,192},{192,224},{224... | collective-permute-start | bytes 196616 | tf_op jit(solution)/shard_map/ppermute | solution.py:19
  252.6 4.7 %collective-permute-start.16 = (f32[32,512]{1,0:T(8,128)S(1)}, f32[32,512]{1,0:T(8,128)S(1)}, u32[]{:S(2)}, u32[]{:S(2)}) collective-permute-start(f32[32,512]{1,0:T(8,128)S(1)} %convert_reduce_fusion), channel_id=1, source_target_pairs={{0,480},{32,0},{64,32},{96,64},{128,96},{160,128},{192,160},{224,1... | collective-permute-start | bytes 196616 | tf_op jit(solution)/shard_map/ppermute | solution.py:24
  259.4 4.6 %collective-permute-start.18 = (f32[32,512]{1,0:T(8,128)S(1)}, f32[32,512]{1,0:T(8,128)S(1)}, u32[]{:S(2)}, u32[]{:S(2)}) collective-permute-start(f32[32,512]{1,0:T(8,128)S(1)} %collective-permute-done.16), channel_id=1, source_target_pairs={{0,480},{32,0},{64,32},{96,64},{128,96},{160,128},{192,160},{224,1... | collective-permute-start | bytes 196616 | tf_op jit(solution)/shard_map/ppermute | solution.py:24
  265.9 4.6 %collective-permute-start.20 = (f32[32,512]{1,0:T(8,128)S(1)}, f32[32,512]{1,0:T(8,128)S(1)}, u32[]{:S(2)}, u32[]{:S(2)}) collective-permute-start(f32[32,512]{1,0:T(8,128)S(1)} %collective-permute-done.18), channel_id=1, source_target_pairs={{0,480},{32,0},{64,32},{96,64},{128,96},{160,128},{192,160},{224,1... | collective-permute-start | bytes 196616 | tf_op jit(solution)/shard_map/ppermute | solution.py:24
  272.5 4.6 %collective-permute-start.22 = (f32[32,512]{1,0:T(8,128)S(1)}, f32[32,512]{1,0:T(8,128)S(1)}, u32[]{:S(2)}, u32[]{:S(2)}) collective-permute-start(f32[32,512]{1,0:T(8,128)S(1)} %collective-permute-done.20), channel_id=1, source_target_pairs={{0,480},{32,0},{64,32},{96,64},{128,96},{160,128},{192,160},{224,1... | collective-permute-start | bytes 196616 | tf_op jit(solution)/shard_map/ppermute | solution.py:24
  279.1 4.6 %collective-permute-start.24 = (f32[32,512]{1,0:T(8,128)S(1)}, f32[32,512]{1,0:T(8,128)S(1)}, u32[]{:S(2)}, u32[]{:S(2)}) collective-permute-start(f32[32,512]{1,0:T(8,128)S(1)} %collective-permute-done.22), channel_id=1, source_target_pairs={{0,480},{32,0},{64,32},{96,64},{128,96},{160,128},{192,160},{224,1... | collective-permute-start | bytes 196616 | tf_op jit(solution)/shard_map/ppermute | solution.py:24
  286.2 4.6 %collective-permute-start.26 = (f32[32,512]{1,0:T(8,128)S(1)}, f32[32,512]{1,0:T(8,128)S(1)}, u32[]{:S(2)}, u32[]{:S(2)}) collective-permute-start(f32[32,512]{1,0:T(8,128)S(1)} %collective-permute-done.24), channel_id=1, source_target_pairs={{0,480},{32,0},{64,32},{96,64},{128,96},{160,128},{192,160},{224,1... | collective-permute-start | bytes 196616 | tf_op jit(solution)/shard_map/ppermute | solution.py:24
  292.8 4.6 %collective-permute-start.28 = (f32[32,512]{1,0:T(8,128)S(1)}, f32[32,512]{1,0:T(8,128)S(1)}, u32[]{:S(2)}, u32[]{:S(2)}) collective-permute-start(f32[32,512]{1,0:T(8,128)S(1)} %collective-permute-done.26), channel_id=1, source_target_pairs={{0,480},{32,0},{64,32},{96,64},{128,96},{160,128},{192,160},{224,1... | collective-permute-start | bytes 196616 | tf_op jit(solution)/shard_map/ppermute | solution.py:24
  305.8 34.7 %all-gather.3 = f32[1024,32]{1,0:T(8,128)S(1)} all-gather(f32[32,32]{1,0:T(8,128)S(1)} %copy.19), channel_id=5, replica_groups=mesh['aux'=16,'pair'=32] {'pair'}, dimensions={0}, use_global_device_ids=true | all-gather | bytes 135168 | tf_op jit(solution)/shard_map/all_gather | solution.py:48
  (145 shorter events, 84.5 us)
Async XLA Ops:
  46.4 35.5 %all-to-all-start = ((bf16[32,16,512]{2,0,1:T(8,128)(2,1)}), bf16[32,16,512]{2,0,1:T(8,128)(2,1)}, u32[]{:S(2)}, u32[]{:S(2)}) async-start(bf16[32,16,512]{2,0,1:T(8,128)(2,1)} %bitcast.63), calls=%async_computation | async-start | bytes 1048576 | tf_op jit(solution)/shard_map/all_to_all | solution.py:55
  83.2 11.1 %collective-permute-start = (f32[32,512]{1,0:T(8,128)S(1)}, f32[32,512]{1,0:T(8,128)S(1)}, u32[]{:S(2)}, u32[]{:S(2)}) collective-permute-start(f32[32,512]{1,0:T(8,128)S(1)} %convert_reduce_fusion.1), channel_id=1, source_target_pairs={{0,32},{32,64},{64,96},{96,128},{128,160},{160,192},{192,224},{224... | collective-permute-start | bytes 196616 | tf_op jit(solution)/shard_map/ppermute | solution.py:19
  89.4 6.7 %collective-permute-start.1 = (f32[32,512]{1,0:T(8,128)S(1)}, f32[32,512]{1,0:T(8,128)S(1)}, u32[]{:S(2)}, u32[]{:S(2)}) collective-permute-start(f32[32,512]{1,0:T(8,128)S(1)} %convert_reduce_fusion.1), channel_id=1, source_target_pairs={{0,480},{32,0},{64,32},{96,64},{128,96},{160,128},{192,160},{224,1... | collective-permute-start | bytes 196616 | tf_op jit(solution)/shard_map/ppermute | solution.py:24
  94.2 6.6 %collective-permute-start.2 = (f32[32,512]{1,0:T(8,128)S(1)}, f32[32,512]{1,0:T(8,128)S(1)}, u32[]{:S(2)}, u32[]{:S(2)}) collective-permute-start(f32[32,512]{1,0:T(8,128)S(1)} %collective-permute-done), channel_id=1, source_target_pairs={{0,32},{32,64},{64,96},{96,128},{128,160},{160,192},{192,224},{224... | collective-permute-start | bytes 196616 | tf_op jit(solution)/shard_map/ppermute | solution.py:19
  96.2 6.6 %collective-permute-start.3 = (f32[32,512]{1,0:T(8,128)S(1)}, f32[32,512]{1,0:T(8,128)S(1)}, u32[]{:S(2)}, u32[]{:S(2)}) collective-permute-start(f32[32,512]{1,0:T(8,128)S(1)} %collective-permute-done.1), channel_id=1, source_target_pairs={{0,480},{32,0},{64,32},{96,64},{128,96},{160,128},{192,160},{224,1... | collective-permute-start | bytes 196616 | tf_op jit(solution)/shard_map/ppermute | solution.py:24
  100.8 6.6 %collective-permute-start.4 = (f32[32,512]{1,0:T(8,128)S(1)}, f32[32,512]{1,0:T(8,128)S(1)}, u32[]{:S(2)}, u32[]{:S(2)}) collective-permute-start(f32[32,512]{1,0:T(8,128)S(1)} %collective-permute-done.2), channel_id=1, source_target_pairs={{0,32},{32,64},{64,96},{96,128},{128,160},{160,192},{192,224},{224... | collective-permute-start | bytes 196616 | tf_op jit(solution)/shard_map/ppermute | solution.py:19
  102.7 6.6 %collective-permute-start.5 = (f32[32,512]{1,0:T(8,128)S(1)}, f32[32,512]{1,0:T(8,128)S(1)}, u32[]{:S(2)}, u32[]{:S(2)}) collective-permute-start(f32[32,512]{1,0:T(8,128)S(1)} %collective-permute-done.3), channel_id=1, source_target_pairs={{0,480},{32,0},{64,32},{96,64},{128,96},{160,128},{192,160},{224,1... | collective-permute-start | bytes 196616 | tf_op jit(solution)/shard_map/ppermute | solution.py:24
  107.4 6.6 %collective-permute-start.6 = (f32[32,512]{1,0:T(8,128)S(1)}, f32[32,512]{1,0:T(8,128)S(1)}, u32[]{:S(2)}, u32[]{:S(2)}) collective-permute-start(f32[32,512]{1,0:T(8,128)S(1)} %collective-permute-done.4), channel_id=1, source_target_pairs={{0,32},{32,64},{64,96},{96,128},{128,160},{160,192},{192,224},{224... | collective-permute-start | bytes 196616 | tf_op jit(solution)/shard_map/ppermute | solution.py:19
  109.3 6.6 %collective-permute-start.7 = (f32[32,512]{1,0:T(8,128)S(1)}, f32[32,512]{1,0:T(8,128)S(1)}, u32[]{:S(2)}, u32[]{:S(2)}) collective-permute-start(f32[32,512]{1,0:T(8,128)S(1)} %collective-permute-done.5), channel_id=1, source_target_pairs={{0,480},{32,0},{64,32},{96,64},{128,96},{160,128},{192,160},{224,1... | collective-permute-start | bytes 196616 | tf_op jit(solution)/shard_map/ppermute | solution.py:24
  113.9 7.2 %collective-permute-start.8 = (f32[32,512]{1,0:T(8,128)S(1)}, f32[32,512]{1,0:T(8,128)S(1)}, u32[]{:S(2)}, u32[]{:S(2)}) collective-permute-start(f32[32,512]{1,0:T(8,128)S(1)} %collective-permute-done.6), channel_id=1, source_target_pairs={{0,32},{32,64},{64,96},{96,128},{128,160},{160,192},{192,224},{224... | collective-permute-start | bytes 196616 | tf_op jit(solution)/shard_map/ppermute | solution.py:19
  115.9 7.1 %collective-permute-start.9 = (f32[32,512]{1,0:T(8,128)S(1)}, f32[32,512]{1,0:T(8,128)S(1)}, u32[]{:S(2)}, u32[]{:S(2)}) collective-permute-start(f32[32,512]{1,0:T(8,128)S(1)} %collective-permute-done.7), channel_id=1, source_target_pairs={{0,480},{32,0},{64,32},{96,64},{128,96},{160,128},{192,160},{224,1... | collective-permute-start | bytes 196616 | tf_op jit(solution)/shard_map/ppermute | solution.py:24
  123.0 6.6 %collective-permute-start.11 = (f32[32,512]{1,0:T(8,128)S(1)}, f32[32,512]{1,0:T(8,128)S(1)}, u32[]{:S(2)}, u32[]{:S(2)}) collective-permute-start(f32[32,512]{1,0:T(8,128)S(1)} %collective-permute-done.9), channel_id=1, source_target_pairs={{0,480},{32,0},{64,32},{96,64},{128,96},{160,128},{192,160},{224,1... | collective-permute-start | bytes 196616 | tf_op jit(solution)/shard_map/ppermute | solution.py:24
  127.7 6.6 %collective-permute-start.12 = (f32[32,512]{1,0:T(8,128)S(1)}, f32[32,512]{1,0:T(8,128)S(1)}, u32[]{:S(2)}, u32[]{:S(2)}) collective-permute-start(f32[32,512]{1,0:T(8,128)S(1)} %collective-permute-done.10), channel_id=1, source_target_pairs={{0,32},{32,64},{64,96},{96,128},{128,160},{160,192},{192,224},{224... | collective-permute-start | bytes 196616 | tf_op jit(solution)/shard_map/ppermute | solution.py:19
  129.6 6.6 %collective-permute-start.13 = (f32[32,512]{1,0:T(8,128)S(1)}, f32[32,512]{1,0:T(8,128)S(1)}, u32[]{:S(2)}, u32[]{:S(2)}) collective-permute-start(f32[32,512]{1,0:T(8,128)S(1)} %collective-permute-done.11), channel_id=1, source_target_pairs={{0,480},{32,0},{64,32},{96,64},{128,96},{160,128},{192,160},{224,1... | collective-permute-start | bytes 196616 | tf_op jit(solution)/shard_map/ppermute | solution.py:24
  219.0 27.2 %all-to-all-start.1 = ((bf16[32,16,512]{2,0,1:T(8,128)(2,1)}), bf16[32,16,512]{2,0,1:T(8,128)(2,1)S(1)}, u32[]{:S(2)}, u32[]{:S(2)}) async-start(bf16[32,16,512]{2,0,1:T(8,128)(2,1)} %bitcast.64), calls=%async_computation.1 | async-start | bytes 1048576 | tf_op jit(solution)/shard_map/all_to_all | solution.py:55
  246.2 11.2 %collective-permute-start.15 = (f32[32,512]{1,0:T(8,128)S(1)}, f32[32,512]{1,0:T(8,128)S(1)}, u32[]{:S(2)}, u32[]{:S(2)}) collective-permute-start(f32[32,512]{1,0:T(8,128)S(1)} %convert_reduce_fusion), channel_id=1, source_target_pairs={{0,32},{32,64},{64,96},{96,128},{128,160},{160,192},{192,224},{224... | collective-permute-start | bytes 196616 | tf_op jit(solution)/shard_map/ppermute | solution.py:19
  252.6 6.8 %collective-permute-start.16 = (f32[32,512]{1,0:T(8,128)S(1)}, f32[32,512]{1,0:T(8,128)S(1)}, u32[]{:S(2)}, u32[]{:S(2)}) collective-permute-start(f32[32,512]{1,0:T(8,128)S(1)} %convert_reduce_fusion), channel_id=1, source_target_pairs={{0,480},{32,0},{64,32},{96,64},{128,96},{160,128},{192,160},{224,1... | collective-permute-start | bytes 196616 | tf_op jit(solution)/shard_map/ppermute | solution.py:24
  257.4 6.6 %collective-permute-start.17 = (f32[32,512]{1,0:T(8,128)S(1)}, f32[32,512]{1,0:T(8,128)S(1)}, u32[]{:S(2)}, u32[]{:S(2)}) collective-permute-start(f32[32,512]{1,0:T(8,128)S(1)} %collective-permute-done.15), channel_id=1, source_target_pairs={{0,32},{32,64},{64,96},{96,128},{128,160},{160,192},{192,224},{224... | collective-permute-start | bytes 196616 | tf_op jit(solution)/shard_map/ppermute | solution.py:19
  259.4 6.6 %collective-permute-start.18 = (f32[32,512]{1,0:T(8,128)S(1)}, f32[32,512]{1,0:T(8,128)S(1)}, u32[]{:S(2)}, u32[]{:S(2)}) collective-permute-start(f32[32,512]{1,0:T(8,128)S(1)} %collective-permute-done.16), channel_id=1, source_target_pairs={{0,480},{32,0},{64,32},{96,64},{128,96},{160,128},{192,160},{224,1... | collective-permute-start | bytes 196616 | tf_op jit(solution)/shard_map/ppermute | solution.py:24
  264.0 6.6 %collective-permute-start.19 = (f32[32,512]{1,0:T(8,128)S(1)}, f32[32,512]{1,0:T(8,128)S(1)}, u32[]{:S(2)}, u32[]{:S(2)}) collective-permute-start(f32[32,512]{1,0:T(8,128)S(1)} %collective-permute-done.17), channel_id=1, source_target_pairs={{0,32},{32,64},{64,96},{96,128},{128,160},{160,192},{192,224},{224... | collective-permute-start | bytes 196616 | tf_op jit(solution)/shard_map/ppermute | solution.py:19
  277.1 7.2 %collective-permute-start.23 = (f32[32,512]{1,0:T(8,128)S(1)}, f32[32,512]{1,0:T(8,128)S(1)}, u32[]{:S(2)}, u32[]{:S(2)}) collective-permute-start(f32[32,512]{1,0:T(8,128)S(1)} %collective-permute-done.21), channel_id=1, source_target_pairs={{0,32},{32,64},{64,96},{96,128},{128,160},{160,192},{192,224},{224... | collective-permute-start | bytes 196616 | tf_op jit(solution)/shard_map/ppermute | solution.py:19
  279.1 7.1 %collective-permute-start.24 = (f32[32,512]{1,0:T(8,128)S(1)}, f32[32,512]{1,0:T(8,128)S(1)}, u32[]{:S(2)}, u32[]{:S(2)}) collective-permute-start(f32[32,512]{1,0:T(8,128)S(1)} %collective-permute-done.22), channel_id=1, source_target_pairs={{0,480},{32,0},{64,32},{96,64},{128,96},{160,128},{192,160},{224,1... | collective-permute-start | bytes 196616 | tf_op jit(solution)/shard_map/ppermute | solution.py:24
  286.2 6.6 %collective-permute-start.26 = (f32[32,512]{1,0:T(8,128)S(1)}, f32[32,512]{1,0:T(8,128)S(1)}, u32[]{:S(2)}, u32[]{:S(2)}) collective-permute-start(f32[32,512]{1,0:T(8,128)S(1)} %collective-permute-done.24), channel_id=1, source_target_pairs={{0,480},{32,0},{64,32},{96,64},{128,96},{160,128},{192,160},{224,1... | collective-permute-start | bytes 196616 | tf_op jit(solution)/shard_map/ppermute | solution.py:24
  292.8 6.6 %collective-permute-start.28 = (f32[32,512]{1,0:T(8,128)S(1)}, f32[32,512]{1,0:T(8,128)S(1)}, u32[]{:S(2)}, u32[]{:S(2)}) collective-permute-start(f32[32,512]{1,0:T(8,128)S(1)} %collective-permute-done.26), channel_id=1, source_target_pairs={{0,480},{32,0},{64,32},{96,64},{128,96},{160,128},{192,160},{224,1... | collective-permute-start | bytes 196616 | tf_op jit(solution)/shard_map/ppermute | solution.py:24
  (18 other events, 224.7 us)
